TPU v7x, 256 devices: a whole 4x4x8 slice. The times are simulated.
256 devices in a mesh: frame: 16 (over z_lo, y), tensor: 8 (over z_hi, x), dp: 2 (over core).
Axes of the slice: x: 4, y: 4, z: 8 (z_hi: 2, z_lo: 4; z = z_hi * 4 + z_lo), core: 2. Of those that a mesh axis runs over, the one named last changes fastest.
Arguments:
- q_proj: bfloat16 [16384, 3072], P(('dp', 'frame'), 'tensor'), parts along dimension 0
- k_proj: bfloat16 [16384, 3072], P(('dp', 'frame'), 'tensor'), parts along dimension 0
- v_proj: bfloat16 [16384, 3072], P(('dp', 'frame'), 'tensor'), parts along dimension 0, may hold values from -6 to 6
- gain_q: float32 [3072], P('tensor'), may hold values from 0.5 to 6
- gain_k: float32 [3072], P('tensor'), may hold values from 0.5 to 6
- tiles: int32 [128, 12], P('dp'), parts along dimension 0, may hold values from 0 to 63, as said below
Outputs:
- attended: bfloat16 [16384, 3072], P(('dp', 'frame'), 'tensor'), parts along dimension 0
There are 2 independent parts, one for each index of `dp`. A program takes and returns all parts, laid end to end along the dimension named above; an argument that names none is the same for every part. Nothing has to cross between parts.
Inputs may be any that keep to these rules, and one draw needn't show every extreme that they name: `tiles`: row q lists 12 distinct key blocks: q first; then 8 blocks whose slab (group of 4 consecutive blocks, one frame slab) is at most 2 slabs from the slab of q; then 3 blocks that are each the first block of a slab more than 2 slabs away. Farther groups are listed less often.
All inputs are finite; a program needn't handle non-finite values.
Results may differ from a plain program's by a relative error of at most 0.007.
The roundings to bfloat16 on the way count: a program that leaves them out, or rounds other values in their place, can miss the bound.
Values may be sent and summed in bfloat16 or wider, within the bound.
No kernel may reach another device: no remote copies, remote signals or barrier semaphores. Data moves between devices by JAX's collectives and lax.ppermute only.
A program may use at most 128 MiB of HBM per device.

v0:
```python
import math

import jax
import jax.numpy as jnp
from jax import lax
from jax.sharding import PartitionSpec as P

HD = 128
BLK = 128


EPS = 1e-06


def attend(state_now, q_heads, keys, values, key_ids, q_tiles):
    run_max, run_sum, run_acc = state_now
    head_count = run_max.shape[0]
    tok_rows = q_heads.shape[0]
    length = keys.shape[0]
    k_heads = keys.reshape(length, head_count, HD)
    v_heads = values.reshape(length, head_count, HD)
    scores = jnp.einsum("qhd,khd->hqk", q_heads, k_heads, preferred_element_type=jnp.float32) * (
        1.0 / math.sqrt(HD)
    )
    listed = jnp.any(q_tiles[:, :, None] == key_ids[None, None, :], axis=1)
    listed = jnp.repeat(listed, tok_rows // q_tiles.shape[0], axis=0)[None]
    scores = jnp.where(listed, scores, -1e30)
    new_max = jnp.maximum(run_max, jnp.max(scores, axis=-1))
    factor = jnp.exp(run_max - new_max)
    weights = jnp.where(listed, jnp.exp(scores - new_max[..., None]), 0.0)
    new_sum = run_sum * factor + jnp.sum(weights, axis=-1)
    product = jnp.einsum(
        "hqk,khd->hqd", weights.astype(jnp.bfloat16), v_heads, preferred_element_type=jnp.float32
    )
    new_acc = run_acc * factor[..., None] + product
    return (new_max, new_sum, new_acc)


def sweep(state_now, q_heads, keys, values, key_ids, q_tiles):
    length = keys.shape[0]
    sub_rows = math.gcd(length, 512)
    steps_count = length // sub_rows
    width = keys.shape[1]
    inputs = (
        keys.reshape(steps_count, sub_rows, width),
        values.reshape(steps_count, sub_rows, width),
        key_ids.reshape(steps_count, sub_rows),
    )

    def one_step(carried, parts_now):
        return (attend(carried, q_heads, parts_now[0], parts_now[1], parts_now[2], q_tiles), None)

    final_state, unused = lax.scan(one_step, state_now, inputs)
    return final_state


def body(q_proj, k_proj, v_proj, gain_q, gain_k, tiles):
    tok_rows, width = q_proj.shape
    head_count = width // HD
    q_wide = q_proj.astype(jnp.float32)
    k_wide = k_proj.astype(jnp.float32)
    row_sums = lax.psum(
        (jnp.sum(q_wide * q_wide, axis=1), jnp.sum(k_wide * k_wide, axis=1)), "tensor"
    )
    full_width = width * lax.axis_size("tensor")
    q_norm = (q_wide * lax.rsqrt(row_sums[0] / full_width + EPS)[:, None] * gain_q).astype(
        jnp.bfloat16
    )
    k_norm = (k_wide * lax.rsqrt(row_sums[1] / full_width + EPS)[:, None] * gain_k).astype(
        jnp.bfloat16
    )
    blocks = tok_rows // BLK
    frame_pos = lax.axis_index("frame")
    q_tiles = lax.dynamic_slice_in_dim(tiles, frame_pos * blocks, blocks, 0)
    q_heads = q_norm.reshape(tok_rows, head_count, HD)
    kv_pair = jnp.stack([k_norm, v_proj])
    state_now = (
        jnp.full((head_count, tok_rows), -1e30, jnp.float32),
        jnp.zeros((head_count, tok_rows), jnp.float32),
        jnp.zeros((head_count, tok_rows, HD), jnp.float32),
    )
    portion = lax.all_gather(kv_pair, "frame", axis=1, tiled=True)
    length = portion.shape[1]
    key_ids = jnp.arange(length, dtype=jnp.int32) // BLK
    state_now = sweep(state_now, q_heads, portion[0], portion[1], key_ids, q_tiles)
    run_max, run_sum, run_acc = state_now
    result = run_acc / run_sum[..., None]
    return jnp.transpose(result, (1, 0, 2)).reshape(tok_rows, width).astype(jnp.bfloat16)


def solution(mesh):
    return jax.shard_map(
        body,
        mesh=mesh,
        in_specs=(
            P(("dp", "frame"), "tensor"),
            P(("dp", "frame"), "tensor"),
            P(("dp", "frame"), "tensor"),
            P("tensor"),
            P("tensor"),
            P("dp", None),
        ),
        out_specs=P(("dp", "frame"), "tensor"),
        check_vma=False,
    )
```

profile of v0, /device:TPU:64, one launch (start us, length us, event | category | flops | bytes accessed | tf_op | source)
XLA Modules:
  0.0 411.6 jit_solution(15182845750359665627)
XLA Ops:
  9.0 31.3 %all-reduce = (f32[512]{0:T(512)S(1)}, f32[512]{0:T(512)S(1)}) all-reduce(f32[512]{0:T(512)S(1)} %fusion.13, f32[512]{0:T(512)S(1)} %fusion.16), channel_id=1, replica_groups=mesh['frame'=16,'tensor'=8,'dp'=2] {'tensor'}, use_global_device_ids=true, to_apply=%region_1.0 | all-reduce | flops 1024 | bytes 8192 | tf_op jit(solution)/shard_map/psum | solution.py:62
  41.5 2.0 pad_maximum_fusion
  44.8 136.8 %all-gather.2.cloned.1.call-done = bf16[2,8192,384]{2,1,0:T(8,128)(2,1)} async-done(((bf16[2,512,384]{2,1,0:T(8,128)(2,1)}), bf16[2,8192,384]{2,1,0:T(8,128)(2,1)}) %all-gather.2.cloned.1.call-update) | async-done | bytes 12582928 | tf_op jit(solution)/shard_map/all_gather | solution.py:82
  181.5 10.2 %fusion.23 = (bf16[1,8192,384]{2,1,0:T(8,128)(2,1)}, bf16[1,8192,384]{2,1,0:T(8,128)(2,1)}) fusion(bf16[2,8192,384]{2,1,0:T(8,128)(2,1)} %all-gather.2.cloned.1.call-done), kind=kLoop, calls=%fused_computation.46 | loop fusion | bytes 25165824 | tf_op jit(solution)/shard_map/slice | solution.py:85
  191.8 210.6 %while.15 = (s32[]{:T(128)}, f32[3,512]{1,0:T(4,128)S(1)}, f32[3,512]{1,0:T(4,128)S(1)}, f32[3,512,128]{2,1,0:T(8,128)}, s32[4,12]{0,1:T(8,128)S(1)}, /*index=5*...) while((s32[]{:T(128)}, f32[3,512]{1,0:T(4,128)S(1)}, ...), condition=%wide.region_8.9_spmd.clone, body=%wide.region_4.8_spmd.clone.sunk | while | flops 413521408 | bytes 17021248 | solution.py:53
  201.5 3.2 fusion.42
  209.6 2.0 fusion.39
  214.4 3.5 fusion.42
  222.8 2.0 fusion.39
  227.6 3.5 fusion.42
  236.0 2.0 fusion.39
  240.7 3.5 fusion.42
  253.9 3.5 fusion.42
  262.3 2.0 fusion.39
  267.1 3.5 fusion.42
  275.5 2.0 fusion.39
  280.3 3.5 fusion.42
  288.7 2.0 fusion.39
  293.4 3.5 fusion.42
  301.9 2.0 fusion.39
  306.6 3.5 fusion.42
  315.1 2.0 fusion.39
  319.8 3.5 fusion.42
  333.0 3.5 fusion.42
  341.4 2.0 fusion.39
  346.2 3.5 fusion.42
  359.3 3.5 fusion.42
  367.8 2.0 fusion.39
  372.5 3.5 fusion.42
  385.7 3.5 fusion.42
  394.1 2.0 fusion.39
  398.9 3.5 fusion.42
  (218 shorter events, 139.7 us)
Async XLA Ops:
  6.5 38.1 %copy-start = (s32[64,12]{0,1:T(8,128)S(1)}, s32[64,12]{0,1:T(8,128)}, u32[]{:S(2)}) copy-start(s32[64,12]{0,1:T(8,128)} %param.13) | copy-start | bytes 9220
  6.5 37.1 %copy-start.1 = (f32[384]{0:T(512)S(1)}, f32[384]{0:T(512)}, u32[]{:S(2)}) copy-start(f32[384]{0:T(512)} %param.11) | copy-start | bytes 4612
  6.5 175.0 %all-gather.2.cloned.1.call-start = ((), (), s32[]{:S(2)}) async-start(), calls=%async_computation | async-start | bytes 13369344 | tf_op jit(solution)/shard_map/all_gather | solution.py:82
Sparse Core Ops, SparseCore 0:
  43.7 137.8 all-gather.1
where the time goes:
time: 418 us; the launch traced here: 412 us
  waiting for transfers between devices  137 us (33%)
  local copies, waits for them, and re-layouts  122 us (29%)
  matrix products  87 us (21%)
  blocking collectives  31.3 us (7%)
  other arithmetic  19.6 us (5%)
  between operations  13.5 us (3%)
    all_gather x1, waiting for transfers between devices, body(): portion = lax.all_gather(kv_pair, 'frame', axis=1, tiled=True)  137 us
    dynamic_slice x64, local copies, waits for them, and re-layouts, sweep(): final_state, unused = lax.scan(one_step, state_now, inputs)  76.9 us
    dot_general x16, matrix products, attend(): jnp.einsum('hqk,khd->hqd', weights.astype(jnp.bfloat16), v_heads, preferr...  55.6 us
    dot_general x16, matrix products, attend(): jnp.einsum('qhd,khd->hqk', q_heads, k_heads, preferred_element_type=jnp.f...  31.5 us
    psum x1, blocking collectives, body(): lax.psum((jnp.sum(q_wide * q_wide, axis=1), jnp.sum(k_wide * k_wide, axis...  31.3 us
    broadcast_in_dim x16, local copies, waits for them, and re-layouts, attend(): listed = jnp.repeat(listed, tok_rows // q_tiles.shape[0], axis=0)[None]  25.6 us
    reduce_sum x16, other arithmetic, attend(): new_sum = run_sum * factor + jnp.sum(weights, axis=-1)  12.9 us
    slice x1, local copies, waits for them, and re-layouts, body(): portion[1]  10.2 us
  transfers between devices with their start and end apart: 1, of which 1 were waited for; matrix products, arithmetic and copies ran while one was open for 0% of the time, Pallas kernels for 0%

commit v1 on v0

v1 whole, which is shorter than its diff:
```python
import functools
import math

import jax
import jax.numpy as jnp
from jax import lax
from jax.experimental import pallas as pl
from jax.experimental.pallas import tpu as pltpu
from jax.sharding import PartitionSpec as P

HD = 128
BLK = 128
NEAR = 2

EPS = 1e-06


def attn_kernel(idx_ref, q_ref, k_ref, v_ref, o_ref, s_ref, *, heads, slots):
    i = pl.program_id(0)
    scale = 1.0 / math.sqrt(HD)
    for h in range(heads):
        cols = pl.ds(h * HD, HD)
        qh = q_ref[:, cols]
        top = None
        for j in range(slots):
            kb = idx_ref[i, j]
            kh = k_ref[kb, :, cols]
            s = lax.dot_general(
                qh, kh, (((1,), (1,)), ((), ())), preferred_element_type=jnp.float32
            ) * scale
            s_ref[j] = s
            part = jnp.max(s, axis=1, keepdims=True)
            top = part if top is None else jnp.maximum(top, part)
        total = None
        acc = None
        for j in range(slots):
            kb = idx_ref[i, j]
            w = jnp.exp(s_ref[j] - top)
            part = jnp.sum(w, axis=1, keepdims=True)
            total = part if total is None else total + part
            prod = jnp.dot(
                w.astype(jnp.bfloat16), v_ref[kb, :, cols], preferred_element_type=jnp.float32
            )
            acc = prod if acc is None else acc + prod
        o_ref[:, cols] = (acc / total).astype(o_ref.dtype)


def sparse_attend(idx, qn, k_bank, v_bank):
    tok_rows, width = qn.shape
    heads = width // HD
    q_blocks = tok_rows // BLK
    slots = idx.shape[1]
    n_bank = k_bank.shape[0]
    kernel = functools.partial(attn_kernel, heads=heads, slots=slots)
    grid_spec = pltpu.PrefetchScalarGridSpec(
        num_scalar_prefetch=1,
        grid=(q_blocks,),
        in_specs=[
            pl.BlockSpec((BLK, width), lambda i, idx_ref: (i, 0)),
            pl.BlockSpec((n_bank, BLK, width), lambda i, idx_ref: (0, 0, 0)),
            pl.BlockSpec((n_bank, BLK, width), lambda i, idx_ref: (0, 0, 0)),
        ],
        out_specs=pl.BlockSpec((BLK, width), lambda i, idx_ref: (i, 0)),
        scratch_shapes=[pltpu.VMEM((slots, BLK, BLK), jnp.float32)],
    )
    flops = 4 * q_blocks * slots * heads * BLK * BLK * HD
    return pl.pallas_call(
        kernel,
        grid_spec=grid_spec,
        out_shape=jax.ShapeDtypeStruct((tok_rows, width), jnp.bfloat16),
        compiler_params=pltpu.CompilerParams(vmem_limit_bytes=48 * 1024 * 1024),
        cost_estimate=pl.CostEstimate(
            flops=flops,
            transcendentals=q_blocks * slots * heads * BLK * BLK,
            bytes_accessed=2 * (2 * tok_rows * width + 2 * n_bank * BLK * width),
        ),
    )(idx, qn, k_bank, v_bank)


def body(q_proj, k_proj, v_proj, gain_q, gain_k, tiles, *, n_frame):
    tok_rows, width = q_proj.shape
    q_wide = q_proj.astype(jnp.float32)
    k_wide = k_proj.astype(jnp.float32)
    row_sums = lax.psum(
        (jnp.sum(q_wide * q_wide, axis=1), jnp.sum(k_wide * k_wide, axis=1)), "tensor"
    )
    full_width = width * lax.axis_size("tensor")
    q_norm = (q_wide * lax.rsqrt(row_sums[0] / full_width + EPS)[:, None] * gain_q).astype(
        jnp.bfloat16
    )
    k_norm = (k_wide * lax.rsqrt(row_sums[1] / full_width + EPS)[:, None] * gain_k).astype(
        jnp.bfloat16
    )
    blocks = tok_rows // BLK
    frame_pos = lax.axis_index("frame")
    kv_pair = jnp.stack([k_norm, v_proj])

    near = {0: kv_pair}
    for d in range(-NEAR, NEAR + 1):
        if d == 0:
            continue
        perm = [(i, i - d) for i in range(n_frame) if 0 <= i - d < n_frame]
        near[d] = lax.ppermute(kv_pair, "frame", perm)
    far = lax.all_gather(kv_pair[:, :BLK], "frame", axis=0, tiled=False)

    near_k = jnp.concatenate(
        [near[d][0].reshape(blocks, BLK, width) for d in range(-NEAR, NEAR + 1)], axis=0
    )
    near_v = jnp.concatenate(
        [near[d][1].reshape(blocks, BLK, width) for d in range(-NEAR, NEAR + 1)], axis=0
    )
    k_bank = jnp.concatenate([near_k, far[:, 0]], axis=0)
    v_bank = jnp.concatenate([near_v, far[:, 1]], axis=0)
    n_near = (2 * NEAR + 1) * blocks

    q_tiles = lax.dynamic_slice_in_dim(tiles, frame_pos * blocks, blocks, 0)
    key_slab = q_tiles // blocks
    dist = key_slab - frame_pos
    idx = jnp.where(
        jnp.abs(dist) <= NEAR,
        (dist + NEAR) * blocks + q_tiles % blocks,
        n_near + key_slab,
    )
    idx = jnp.clip(idx, 0, n_near + n_frame - 1).astype(jnp.int32)
    return sparse_attend(idx, q_norm, k_bank, v_bank)


def solution(mesh):
    return jax.shard_map(
        functools.partial(body, n_frame=mesh.shape["frame"]),
        mesh=mesh,
        in_specs=(
            P(("dp", "frame"), "tensor"),
            P(("dp", "frame"), "tensor"),
            P(("dp", "frame"), "tensor"),
            P("tensor"),
            P("tensor"),
            P("dp", None),
        ),
        out_specs=P(("dp", "frame"), "tensor"),
        check_vma=False,
    )
```

time: 418 us -> 175 us (0.42); the launches traced: 412 us -> 175 us
  local copies, waits for them, and re-layouts: 122 us -> 10.6 us
  matrix products: 87 us -> 0 us
  waiting for transfers between devices: 137 us -> 85.7 us
  starting transfers between devices: 0.01 us -> 15 us
  other arithmetic: 19.6 us -> 7.26 us
  Pallas kernels: 0 us -> 11.4 us
    all_gather x1, waiting for transfers between devices: 137 us -> 12.9 us  [body(): far = lax.all_gather(kv_pair[:, :BLK], 'frame', axis=0, tiled=False)]
    dot_general x32 -> x0, matrix products: 87 us -> none  [the longest x16 55.6 us: attend(): jnp.einsum('hqk,khd->hqd', weights.astype(jnp.bfloat16), v_heads, preferr...]
    dynamic_slice x64 -> x0, local copies, waits for them, and re-layouts: 76.9 us -> none  [sweep(): final_state, unused = lax.scan(one_step, state_now, inputs)]
    ppermute x0 -> x4, waiting for transfers between devices: none -> 72.8 us  [body(): near[d] = lax.ppermute(kv_pair, 'frame', perm)]
    broadcast_in_dim x16 -> x0, local copies, waits for them, and re-layouts: 25.6 us -> none  [attend(): listed = jnp.repeat(listed, tok_rows // q_tiles.shape[0], axis=0)[None]]
    ppermute x0 -> x4, starting transfers between devices: none -> 15 us  [body(): near[d] = lax.ppermute(kv_pair, 'frame', perm)]
    reduce_sum x17 -> x0, other arithmetic: 14 us -> none  [the longest x16 12.9 us: attend(): new_sum = run_sum * factor + jnp.sum(weights, axis=-1)]
    pallas_call x0 -> x1, Pallas kernels: none -> 11.4 us  [sparse_attend(): pl.pallas_call(kernel, grid_spec=grid_spec, out_shape=jax.ShapeDtypeStruc...]
  transfers between devices with their start and end apart: 1 -> 5, of which waited for: 1 -> 4; matrix products, arithmetic and copies ran while one was open for 0% -> 6% of each run, Pallas kernels for 0% -> 0%
where the time goes in v1:
time: 175 us
  waiting for transfers between devices  85.7 us (49%)
  blocking collectives  31.3 us (18%)
  starting transfers between devices  15 us (9%)
  between operations  13.6 us (8%)
  Pallas kernels  11.4 us (7%)
  local copies, waits for them, and re-layouts  10.6 us (6%)
  other arithmetic  7.26 us (4%)
    ppermute x4, waiting for transfers between devices, body(): near[d] = lax.ppermute(kv_pair, 'frame', perm)  72.8 us
    psum x1, blocking collectives, body(): lax.psum((jnp.sum(q_wide * q_wide, axis=1), jnp.sum(k_wide * k_wide, axis...  31.3 us
    ppermute x4, starting transfers between devices, body(): near[d] = lax.ppermute(kv_pair, 'frame', perm)  15 us
    all_gather x1, waiting for transfers between devices, body(): far = lax.all_gather(kv_pair[:, :BLK], 'frame', axis=0, tiled=False)  12.9 us
    pallas_call x1, Pallas kernels, sparse_attend(): pl.pallas_call(kernel, grid_spec=grid_spec, out_shape=jax.ShapeDtypeStruc...  11.4 us
    another operation x3, other arithmetic, body(): kv_pair = jnp.stack([k_norm, v_proj])  4.74 us
    unnamed x25, local copies, waits for them, and re-layouts  4.36 us
    concatenate x1, local copies, waits for them, and re-layouts, body(): v_bank = jnp.concatenate([near_v, far[:, 1]], axis=0)  3.59 us
  transfers between devices with their start and end apart: 5, of which 4 were waited for; matrix products, arithmetic and copies ran while one was open for 6% of the time, Pallas kernels for 0%

profile of v1, /device:TPU:64, one launch (start us, length us, event | category | flops | bytes accessed | tf_op | source)
XLA Modules:
  0.0 174.8 jit_solution(823073095748514654)
XLA Ops:
  6.6 1.4 fusion.2
  8.0 31.3 %all-reduce = (f32[512]{0:T(512)S(1)}, f32[512]{0:T(512)S(1)}) all-reduce(f32[512]{0:T(512)S(1)} %get-tuple-element.17, f32[512]{0:T(512)S(1)} %get-tuple-element.18), channel_id=1, replica_groups=mesh['frame'=16,'tensor'=8,'dp'=2] {'tensor'}, use_global_device_ids=true, to_apply=%region_1.0 | all-reduce | flops 1024 | bytes 8192 | tf_op jit(solution)/shard_map/psum | solution.py:84
  39.4 1.2 fusion.18
  40.5 1.6 fusion.8
  42.2 2.0 %pad_maximum_fusion = bf16[2,512,384]{2,1,0:T(8,128)(2,1)} fusion(bf16[1,512,384]{2,1,0:T(8,128)(2,1)} %bitcast.27, bf16[1,512,384]{2,1,0:T(8,128)(2,1)S(1)} %fusion.18), kind=kLoop, calls=%fused_computation.9 | loop fusion | flops 393216 | bytes 1572864 | tf_op jit(solution)/shard_map/stack | solution.py:96
  44.1 5.1 %collective-permute-start = (bf16[2,512,384]{2,1,0:T(8,128)(2,1)}, bf16[2,512,384]{2,1,0:T(8,128)(2,1)S(1)}, u32[]{:S(2)}, u32[]{:S(2)}) collective-permute-start(bf16[2,512,384]{2,1,0:T(8,128)(2,1)} %pad_maximum_fusion), channel_id=1, source_target_pairs={{0,32},{16,48},{32,64},{48,80},{64,96},{80,112},{96,128},{112,144}... | collective-permute-start | bytes 2359304 | tf_op jit(solution)/shard_map/ppermute | solution.py:103
  49.2 2.6 %collective-permute-start.1 = (bf16[2,512,384]{2,1,0:T(8,128)(2,1)}, bf16[2,512,384]{2,1,0:T(8,128)(2,1)S(1)}, u32[]{:S(2)}, u32[]{:S(2)}) collective-permute-start(bf16[2,512,384]{2,1,0:T(8,128)(2,1)} %pad_maximum_fusion), channel_id=1, source_target_pairs={{0,16},{16,32},{32,48},{48,64},{64,80},{80,96},{96,112},{112,128},... | collective-permute-start | bytes 2359304 | tf_op jit(solution)/shard_map/ppermute | solution.py:103
  51.8 5.4 %collective-permute-start.2 = (bf16[2,512,384]{2,1,0:T(8,128)(2,1)}, bf16[2,512,384]{2,1,0:T(8,128)(2,1)}, u32[]{:S(2)}, u32[]{:S(2)}) collective-permute-start(bf16[2,512,384]{2,1,0:T(8,128)(2,1)} %pad_maximum_fusion), channel_id=1, source_target_pairs={{16,0},{32,16},{48,32},{64,48},{80,64},{96,80},{112,96},{128,112},... | collective-permute-start | bytes 2359304 | tf_op jit(solution)/shard_map/ppermute | solution.py:103
  57.2 1.9 %collective-permute-start.3 = (bf16[2,512,384]{2,1,0:T(8,128)(2,1)}, bf16[2,512,384]{2,1,0:T(8,128)(2,1)}, u32[]{:S(2)}, u32[]{:S(2)}) collective-permute-start(bf16[2,512,384]{2,1,0:T(8,128)(2,1)} %pad_maximum_fusion), channel_id=1, source_target_pairs={{32,0},{48,16},{64,32},{80,48},{96,64},{112,80},{128,96},{144,112}... | collective-permute-start | bytes 2359304 | tf_op jit(solution)/shard_map/ppermute | solution.py:103
  59.1 0.1 constant_dynamic-slice_fusion
  59.2 0.1 copy.14
  59.4 0.2 fusion.7
  59.6 0.9 fusion.4.q_ref
  60.5 11.1 %collective-permute-done = bf16[2,512,384]{2,1,0:T(8,128)(2,1)S(1)} collective-permute-done((bf16[2,512,384]{2,1,0:T(8,128)(2,1)}, bf16[2,512,384]{2,1,0:T(8,128)(2,1)S(1)}, u32[]{:S(2)}, u32[]{:S(2)}) %collective-permute-start) | collective-permute-done | bytes 786464 | tf_op jit(solution)/shard_map/ppermute | solution.py:103
  71.6 0.1 fusion.17
  71.7 18.6 %collective-permute-done.1 = bf16[2,512,384]{2,1,0:T(8,128)(2,1)S(1)} collective-permute-done((bf16[2,512,384]{2,1,0:T(8,128)(2,1)}, bf16[2,512,384]{2,1,0:T(8,128)(2,1)S(1)}, u32[]{:S(2)}, u32[]{:S(2)}) %collective-permute-start.1) | collective-permute-done | bytes 786464 | tf_op jit(solution)/shard_map/ppermute | solution.py:103
  90.3 0.1 fusion.16
  90.4 0.8 constant_dynamic-update-slice_fusion.9
  91.2 0.1 constant_dynamic-update-slice_fusion.3
  91.2 0.1 constant_dynamic-update-slice_fusion.2
  91.3 43.1 %collective-permute-done.2 = bf16[2,512,384]{2,1,0:T(8,128)(2,1)} collective-permute-done((bf16[2,512,384]{2,1,0:T(8,128)(2,1)}, bf16[2,512,384]{2,1,0:T(8,128)(2,1)}, u32[]{:S(2)}, u32[]{:S(2)}) %collective-permute-start.2) | collective-permute-done | bytes 786464 | tf_op jit(solution)/shard_map/ppermute | solution.py:103
  134.4 1.2 fusion.15
  135.6 0.1 constant_dynamic-update-slice_fusion.1
  135.7 1.2 fusion.14
  136.9 0.1 constant_dynamic-update-slice_fusion
  136.9 0.8 constant_dynamic-update-slice_fusion.8
  137.7 0.8 constant_dynamic-update-slice_fusion.7
  138.5 0.8 constant_dynamic-update-slice_fusion.6
  139.3 0.8 constant_dynamic-update-slice_fusion.5
  140.1 12.9 %all-gather.3.cloned.1.call-done = bf16[32,128,384]{2,1,0:T(8,128)(2,1)} async-done(((bf16[2,128,384]{2,1,0:T(8,128)(2,1)}), bf16[32,128,384]{2,1,0:T(8,128)(2,1)}) %all-gather.3.cloned.1.call-update) | async-done | bytes 3145744 | tf_op jit(solution)/shard_map/all_gather | solution.py:104
  153.0 3.6 %fusion = (bf16[36,128,384]{2,1,0:T(8,128)(2,1)}, bf16[36,128,384]{2,1,0:T(8,128)(2,1)S(1)}) fusion(bf16[36,128,384]{2,1,0:T(8,128)(2,1)} %constant_dynamic-update-slice_fusion.5, bf16[16,2,128,384]{3,2,1,0:T(8,128)(2,1)} %bitcast.29, bf16[36,128,384]{2,1,0:T(8,128)(2,1)S(1)} %constant_dynamic-update-slice_fusion), kind=kLoop, calls=%fused_computation.1 | loop fusion | bytes 6291456 | tf_op jit(solution)/shard_map/concatenate | solution.py:113
  156.6 11.4 %shard_map.64 = bf16[512,384]{1,0:T(8,128)(2,1)} custom-call(s32[4,12]{1,0:T(4,128)S(1)} %fusion.11.idx_ref, bf16[512,384]{1,0:T(8,128)(2,1)S(1)} %copy-done.1, bf16[36,128,384]{2,1,0:T(8,128)(2,1)S(1)} %get-tuple-element.8.k_ref, bf16[36,128,384]{2,1,0:T(8,128)(2,1)} %get-tuple-element.7.v_ref), custom_call_target="tpu_custom_call" | custom-call | flops 1207959552 | bytes 7864320 | tf_op jit(solution)/shard_map/pallas_call | solution.py:67
  (21 shorter events, 0.2 us)
Async XLA Ops:
  6.5 52.6 %copy-start = (s32[64,12]{0,1:T(8,128)S(1)}, s32[64,12]{0,1:T(8,128)}, u32[]{:S(2)}) copy-start(s32[64,12]{0,1:T(8,128)} %param.11) | copy-start | bytes 9220
  6.5 53.0 %copy-start.4 = (bf16[512,384]{1,0:T(8,128)(2,1)S(1)}, bf16[512,384]{1,0:T(8,128)(2,1)}, u32[]{:S(2)}) copy-start(bf16[512,384]{1,0:T(8,128)(2,1)} %param.6) | copy-start | bytes 1179652
  6.5 52.8 %copy-start.2 = (bf16[512,384]{1,0:T(8,128)(2,1)S(1)}, bf16[512,384]{1,0:T(8,128)(2,1)}, u32[]{:S(2)}) copy-start(bf16[512,384]{1,0:T(8,128)(2,1)} %param.7) | copy-start | bytes 1179652
  6.5 52.8 %copy-start.5 = (f32[384]{0:T(512)S(1)}, f32[384]{0:T(512)}, u32[]{:S(2)}) copy-start(f32[384]{0:T(512)} %param.10) | copy-start | bytes 4612
  6.5 53.0 %copy-start.6 = (f32[384]{0:T(512)S(1)}, f32[384]{0:T(512)}, u32[]{:S(2)}) copy-start(f32[384]{0:T(512)} %param.9) | copy-start | bytes 4612
  6.5 146.4 %all-gather.3.cloned.1.call-start = ((), (), s32[]{:S(2)}) async-start(), calls=%async_computation | async-start | bytes 3342336 | tf_op jit(solution)/shard_map/all_gather | solution.py:104
  44.1 27.5 %collective-permute-start = (bf16[2,512,384]{2,1,0:T(8,128)(2,1)}, bf16[2,512,384]{2,1,0:T(8,128)(2,1)S(1)}, u32[]{:S(2)}, u32[]{:S(2)}) collective-permute-start(bf16[2,512,384]{2,1,0:T(8,128)(2,1)} %pad_maximum_fusion), channel_id=1, source_target_pairs={{0,32},{16,48},{32,64},{48,80},{64,96},{80,112},{96,128},{112,144}... | collective-permute-start | bytes 2359304 | tf_op jit(solution)/shard_map/ppermute | solution.py:103
  49.2 41.0 %collective-permute-start.1 = (bf16[2,512,384]{2,1,0:T(8,128)(2,1)}, bf16[2,512,384]{2,1,0:T(8,128)(2,1)S(1)}, u32[]{:S(2)}, u32[]{:S(2)}) collective-permute-start(bf16[2,512,384]{2,1,0:T(8,128)(2,1)} %pad_maximum_fusion), channel_id=1, source_target_pairs={{0,16},{16,32},{32,48},{48,64},{64,80},{80,96},{96,112},{112,128},... | collective-permute-start | bytes 2359304 | tf_op jit(solution)/shard_map/ppermute | solution.py:103
  51.8 82.6 %collective-permute-start.2 = (bf16[2,512,384]{2,1,0:T(8,128)(2,1)}, bf16[2,512,384]{2,1,0:T(8,128)(2,1)}, u32[]{:S(2)}, u32[]{:S(2)}) collective-permute-start(bf16[2,512,384]{2,1,0:T(8,128)(2,1)} %pad_maximum_fusion), channel_id=1, source_target_pairs={{16,0},{32,16},{48,32},{64,48},{80,64},{96,80},{112,96},{128,112},... | collective-permute-start | bytes 2359304 | tf_op jit(solution)/shard_map/ppermute | solution.py:103
  57.2 78.4 %collective-permute-start.3 = (bf16[2,512,384]{2,1,0:T(8,128)(2,1)}, bf16[2,512,384]{2,1,0:T(8,128)(2,1)}, u32[]{:S(2)}, u32[]{:S(2)}) collective-permute-start(bf16[2,512,384]{2,1,0:T(8,128)(2,1)} %pad_maximum_fusion), channel_id=1, source_target_pairs={{32,0},{48,16},{64,32},{80,48},{96,64},{112,80},{128,96},{144,112}... | collective-permute-start | bytes 2359304 | tf_op jit(solution)/shard_map/ppermute | solution.py:103
  91.2 46.5 %copy-start.3 = (bf16[512,384]{1,0:T(8,128)(2,1)S(1)}, bf16[512,384]{1,0:T(8,128)(2,1)}, u32[]{:S(2)}) copy-start(bf16[512,384]{1,0:T(8,128)(2,1)} %param.8) | copy-start | bytes 1179652
  153.0 3.6 %copy-start.1 = (bf16[512,384]{1,0:T(8,128)(2,1)S(1)}, bf16[512,384]{1,0:T(8,128)(2,1)}, u32[]{:S(2)}) copy-start(bf16[512,384]{1,0:T(8,128)(2,1)} %fusion.4.q_ref) | copy-start | bytes 1179652
Sparse Core Ops, SparseCore 0:
  42.3 110.6 all-gather.2

commit v2 on v1

--- a/solution.py
+++ b/solution.py
@@ -7,6 +7,7 @@
 from jax.experimental import pallas as pl
 from jax.experimental.pallas import tpu as pltpu
 from jax.sharding import PartitionSpec as P
+
 
 HD = 128
 BLK = 128
@@ -79,6 +80,22 @@
 
 def body(q_proj, k_proj, v_proj, gain_q, gain_k, tiles, *, n_frame):
     tok_rows, width = q_proj.shape
+    blocks = tok_rows // BLK
+    frame_pos = lax.axis_index("frame")
+    shifts = [d for d in range(-NEAR, NEAR + 1) if d != 0]
+
+    def exchange(arr):
+        tail = arr[BLK:]
+        near = {0: tail}
+        for d in shifts:
+            perm = [(i, i - d) for i in range(n_frame) if 0 <= i - d < n_frame]
+            near[d] = lax.ppermute(tail, "frame", perm)
+        first = lax.all_gather(arr[:BLK], "frame", axis=0, tiled=False)
+        parts = [near[d].reshape(blocks - 1, BLK, width) for d in range(-NEAR, NEAR + 1)]
+        return jnp.concatenate(parts + [first], axis=0)
+
+    v_bank = exchange(v_proj)
+
     q_wide = q_proj.astype(jnp.float32)
     k_wide = k_proj.astype(jnp.float32)
     row_sums = lax.psum(
@@ -91,34 +108,17 @@
     k_norm = (k_wide * lax.rsqrt(row_sums[1] / full_width + EPS)[:, None] * gain_k).astype(
         jnp.bfloat16
     )
-    blocks = tok_rows // BLK
-    frame_pos = lax.axis_index("frame")
-    kv_pair = jnp.stack([k_norm, v_proj])
-
-    near = {0: kv_pair}
-    for d in range(-NEAR, NEAR + 1):
-        if d == 0:
-            continue
-        perm = [(i, i - d) for i in range(n_frame) if 0 <= i - d < n_frame]
-        near[d] = lax.ppermute(kv_pair, "frame", perm)
-    far = lax.all_gather(kv_pair[:, :BLK], "frame", axis=0, tiled=False)
-
-    near_k = jnp.concatenate(
-        [near[d][0].reshape(blocks, BLK, width) for d in range(-NEAR, NEAR + 1)], axis=0
-    )
-    near_v = jnp.concatenate(
-        [near[d][1].reshape(blocks, BLK, width) for d in range(-NEAR, NEAR + 1)], axis=0
-    )
-    k_bank = jnp.concatenate([near_k, far[:, 0]], axis=0)
-    v_bank = jnp.concatenate([near_v, far[:, 1]], axis=0)
-    n_near = (2 * NEAR + 1) * blocks
+    k_bank = exchange(k_norm)
+    n_near = (2 * NEAR + 1) * (blocks - 1)
 
     q_tiles = lax.dynamic_slice_in_dim(tiles, frame_pos * blocks, blocks, 0)
     key_slab = q_tiles // blocks
+    within = q_tiles % blocks
     dist = key_slab - frame_pos
+    near_ok = (jnp.abs(dist) <= NEAR) & (within > 0)
     idx = jnp.where(
-        jnp.abs(dist) <= NEAR,
-        (dist + NEAR) * blocks + q_tiles % blocks,
+        near_ok,
+        (dist + NEAR) * (blocks - 1) + within - 1,
         n_near + key_slab,
     )
     idx = jnp.clip(idx, 0, n_near + n_frame - 1).astype(jnp.int32)

time: 175 us -> 230 us (1.31)
  the two profiles are of different devices: /device:TPU:64 before, /device:TPU:2 now
where the time goes in v2:
time: 230 us
  waiting for transfers between devices  130 us (57%)
  blocking collectives  26.5 us (12%)
  starting transfers between devices  25.6 us (11%)
  local copies, waits for them, and re-layouts  20.1 us (9%)
  between operations  13.5 us (6%)
  Pallas kernels  11.2 us (5%)
  other arithmetic  2.76 us (1%)
    all_gather x2, waiting for transfers between devices, exchange(): first = lax.all_gather(arr[:BLK], 'frame', axis=0, tiled=False)  118 us
    psum x1, blocking collectives, body(): lax.psum((jnp.sum(q_wide * q_wide, axis=1), jnp.sum(k_wide * k_wide, axis...  26.5 us
    ppermute x8, starting transfers between devices, exchange(): near[d] = lax.ppermute(tail, 'frame', perm)  25.6 us
    ppermute x8, waiting for transfers between devices, exchange(): near[d] = lax.ppermute(tail, 'frame', perm)  11.7 us
    pallas_call x1, Pallas kernels, sparse_attend(): pl.pallas_call(kernel, grid_spec=grid_spec, out_shape=jax.ShapeDtypeStruc...  11.2 us
    unnamed x17, local copies, waits for them, and re-layouts  10.8 us
  transfers between devices with their start and end apart: 10, of which 5 were waited for; matrix products, arithmetic and copies ran while one was open for 7% of the time, Pallas kernels for 0%

profile of v2, /device:TPU:2, one launch (start us, length us, event | category | flops | bytes accessed | tf_op | source)
XLA Modules:
  0.0 229.7 jit_solution(14932639354697344808)
XLA Ops:
  6.5 1.4 fusion
  7.9 26.5 %all-reduce = (f32[512]{0:T(512)S(1)}, f32[512]{0:T(512)S(1)}) all-reduce(f32[512]{0:T(512)S(1)} %get-tuple-element.7, f32[512]{0:T(512)S(1)} %get-tuple-element.8), channel_id=1, replica_groups=mesh['frame'=16,'tensor'=8,'dp'=2] {'tensor'}, use_global_device_ids=true, to_apply=%region_1.0 | all-reduce | flops 1024 | bytes 8192 | tf_op jit(solution)/shard_map/psum | solution.py:101
  34.4 1.2 fusion.5
  36.3 1.5 slice.15
  37.9 0.7 slice.16
  38.6 5.8 %collective-permute-start = (bf16[384,384]{1,0:T(8,128)(2,1)}, bf16[384,384]{1,0:T(8,128)(2,1)}, u32[]{:S(2)}, u32[]{:S(2)}) collective-permute-start(bf16[384,384]{1,0:T(8,128)(2,1)} %slice.16), channel_id=1, source_target_pairs={{0,32},{16,48},{32,64},{48,80},{64,96},{80,112},{96,128},{112,144}... | collective-permute-start | bytes 884744 | tf_op jit(solution)/shard_map/ppermute | solution.py:92
  44.4 3.3 %collective-permute-start.1 = (bf16[384,384]{1,0:T(8,128)(2,1)}, bf16[384,384]{1,0:T(8,128)(2,1)}, u32[]{:S(2)}, u32[]{:S(2)}) collective-permute-start(bf16[384,384]{1,0:T(8,128)(2,1)} %slice.16), channel_id=1, source_target_pairs={{0,16},{16,32},{32,48},{48,64},{64,80},{80,96},{96,112},{112,128},... | collective-permute-start | bytes 884744 | tf_op jit(solution)/shard_map/ppermute | solution.py:92
  47.7 1.3 collective-permute-start.2
  49.0 1.3 collective-permute-start.3
  50.3 1.7 slice.14
  52.0 6.8 %collective-permute-start.4 = (bf16[384,384]{1,0:T(8,128)(2,1)}, bf16[384,384]{1,0:T(8,128)(2,1)}, u32[]{:S(2)}, u32[]{:S(2)}) collective-permute-start(bf16[384,384]{1,0:T(8,128)(2,1)} %slice.14), channel_id=1, source_target_pairs={{0,32},{16,48},{32,64},{48,80},{64,96},{80,112},{96,128},{112,144}... | collective-permute-start | bytes 884744 | tf_op jit(solution)/shard_map/ppermute | solution.py:92
  59.2 4.6 %collective-permute-start.5 = (bf16[384,384]{1,0:T(8,128)(2,1)}, bf16[384,384]{1,0:T(8,128)(2,1)S(1)}, u32[]{:S(2)}, u32[]{:S(2)}) collective-permute-start(bf16[384,384]{1,0:T(8,128)(2,1)} %slice.14), channel_id=1, source_target_pairs={{0,16},{16,32},{32,48},{48,64},{64,80},{80,96},{96,112},{112,128},... | collective-permute-start | bytes 884744 | tf_op jit(solution)/shard_map/ppermute | solution.py:92
  63.8 1.0 constant_dynamic-update-slice_fusion.5
  64.8 7.5 %collective-permute-done.4 = bf16[384,384]{1,0:T(8,128)(2,1)} collective-permute-done((bf16[384,384]{1,0:T(8,128)(2,1)}, bf16[384,384]{1,0:T(8,128)(2,1)}, u32[]{:S(2)}, u32[]{:S(2)}) %collective-permute-start.4) | collective-permute-done | bytes 294944 | tf_op jit(solution)/shard_map/ppermute | solution.py:92
  72.3 1.3 collective-permute-start.6
  73.6 1.7 constant_dynamic-update-slice_fusion.11
  75.3 1.3 collective-permute-start.7
  76.6 1.0 constant_dynamic-update-slice_fusion.4
  77.6 1.0 constant_dynamic-update-slice_fusion.3
  78.6 1.0 constant_dynamic-update-slice_fusion.2
  79.6 1.0 constant_dynamic-update-slice_fusion.1
  80.6 0.8 constant_dynamic-update-slice_fusion.10
  81.4 1.7 constant_dynamic-update-slice_fusion.9
  83.1 2.2 collective-permute-done.6
  85.3 0.8 constant_dynamic-update-slice_fusion.8
  86.1 2.0 collective-permute-done.7
  88.1 0.8 constant_dynamic-update-slice_fusion.7
  88.8 37.2 %all-gather.5.cloned.1.call-done = bf16[2048,384]{1,0:T(8,128)(2,1)} async-done(((bf16[128,384]{1,0:T(8,128)(2,1)}), bf16[2048,384]{1,0:T(8,128)(2,1)}) %all-gather.5.cloned.1.call-update) | async-done | bytes 1572880 | tf_op jit(solution)/shard_map/all_gather | solution.py:93
  126.0 1.8 constant_dynamic-update-slice_fusion.k_ref
  127.8 81.1 %all-gather.7.cloned.1.call-done = bf16[2048,384]{1,0:T(8,128)(2,1)} async-done(((bf16[128,384]{1,0:T(8,128)(2,1)}), bf16[2048,384]{1,0:T(8,128)(2,1)}) %all-gather.7.cloned.1.call-update) | async-done | bytes 1572880 | tf_op jit(solution)/shard_map/all_gather | solution.py:93
  208.9 2.8 %constant_dynamic-update-slice_fusion.6.v_ref = bf16[31,128,384]{2,1,0:T(8,128)(2,1)} fusion(bf16[31,128,384]{2,1,0:T(8,128)(2,1)} %constant_dynamic-update-slice_fusion.7, bf16[16,128,384]{2,1,0:T(8,128)(2,1)} %bitcast.13), kind=kLoop, calls=%fused_computation.16 | loop fusion | bytes 3145728 | tf_op jit(solution)/shard_map/concatenate | solution.py:95
  211.6 11.2 %shard_map.64 = bf16[512,384]{1,0:T(8,128)(2,1)} custom-call(s32[4,12]{1,0:T(4,128)S(1)} %select_clamp_fusion.idx_ref, bf16[512,384]{1,0:T(8,128)(2,1)S(1)} %fusion.2.q_ref, bf16[31,128,384]{2,1,0:T(8,128)(2,1)S(1)} %constant_dynamic-update-slice_fusion.k_ref, bf16[31,128,384]{2,1,0:T(8,128)(2,1)} %constant_dynamic-update-slice_fusion.6.v_ref), custom_call_target="tpu_custom_call" | custom-call | flops 1207959552 | bytes 6881280 | tf_op jit(solution)/shard_map/pallas_call | solution.py:68
  (22 shorter events, 1.1 us)
Async XLA Ops:
  6.5 52.4 %copy-start = (s32[64,12]{0,1:T(8,128)S(1)}, s32[64,12]{0,1:T(8,128)}, u32[]{:S(2)}) copy-start(s32[64,12]{0,1:T(8,128)} %param.11) | copy-start | bytes 9220
  6.5 52.3 %copy-start.1 = (bf16[512,384]{1,0:T(8,128)(2,1)S(1)}, bf16[512,384]{1,0:T(8,128)(2,1)}, u32[]{:S(2)}) copy-start(bf16[512,384]{1,0:T(8,128)(2,1)} %param.6) | copy-start | bytes 1179652
  6.5 52.3 %copy-start.2 = (f32[384]{0:T(512)S(1)}, f32[384]{0:T(512)}, u32[]{:S(2)}) copy-start(f32[384]{0:T(512)} %param.9) | copy-start | bytes 4612
  6.5 119.5 %all-gather.5.cloned.1.call-start = ((), (), s32[]{:S(2)}) async-start(), calls=%async_computation | async-start | bytes 1671168 | tf_op jit(solution)/shard_map/all_gather | solution.py:93
  36.2 172.6 %all-gather.7.cloned.1.call-start = ((), (), s32[]{:S(2)}) async-start(), calls=%async_computation.1 | async-start | bytes 1671168 | tf_op jit(solution)/shard_map/all_gather | solution.py:93
  38.6 20.6 %collective-permute-start = (bf16[384,384]{1,0:T(8,128)(2,1)}, bf16[384,384]{1,0:T(8,128)(2,1)}, u32[]{:S(2)}, u32[]{:S(2)}) collective-permute-start(bf16[384,384]{1,0:T(8,128)(2,1)} %slice.16), channel_id=1, source_target_pairs={{0,32},{16,48},{32,64},{48,80},{64,96},{80,112},{96,128},{112,144}... | collective-permute-start | bytes 884744 | tf_op jit(solution)/shard_map/ppermute | solution.py:92
  44.4 30.9 %collective-permute-start.1 = (bf16[384,384]{1,0:T(8,128)(2,1)}, bf16[384,384]{1,0:T(8,128)(2,1)}, u32[]{:S(2)}, u32[]{:S(2)}) collective-permute-start(bf16[384,384]{1,0:T(8,128)(2,1)} %slice.16), channel_id=1, source_target_pairs={{0,16},{16,32},{32,48},{48,64},{64,80},{80,96},{96,112},{112,128},... | collective-permute-start | bytes 884744 | tf_op jit(solution)/shard_map/ppermute | solution.py:92
  47.7 30.9 %collective-permute-start.2 = (bf16[384,384]{1,0:T(8,128)(2,1)}, bf16[384,384]{1,0:T(8,128)(2,1)}, u32[]{:S(2)}, u32[]{:S(2)}) collective-permute-start(bf16[384,384]{1,0:T(8,128)(2,1)} %slice.16), channel_id=1, source_target_pairs={{16,0},{32,16},{48,32},{64,48},{80,64},{96,80},{112,96},{128,112},... | collective-permute-start | bytes 884744 | tf_op jit(solution)/shard_map/ppermute | solution.py:92
  49.0 30.6 %collective-permute-start.3 = (bf16[384,384]{1,0:T(8,128)(2,1)}, bf16[384,384]{1,0:T(8,128)(2,1)}, u32[]{:S(2)}, u32[]{:S(2)}) collective-permute-start(bf16[384,384]{1,0:T(8,128)(2,1)} %slice.16), channel_id=1, source_target_pairs={{32,0},{48,16},{64,32},{80,48},{96,64},{112,80},{128,96},{144,112}... | collective-permute-start | bytes 884744 | tf_op jit(solution)/shard_map/ppermute | solution.py:92
  52.0 20.2 %collective-permute-start.4 = (bf16[384,384]{1,0:T(8,128)(2,1)}, bf16[384,384]{1,0:T(8,128)(2,1)}, u32[]{:S(2)}, u32[]{:S(2)}) collective-permute-start(bf16[384,384]{1,0:T(8,128)(2,1)} %slice.14), channel_id=1, source_target_pairs={{0,32},{16,48},{32,64},{48,80},{64,96},{80,112},{96,128},{112,144}... | collective-permute-start | bytes 884744 | tf_op jit(solution)/shard_map/ppermute | solution.py:92
  59.2 21.5 %collective-permute-start.5 = (bf16[384,384]{1,0:T(8,128)(2,1)}, bf16[384,384]{1,0:T(8,128)(2,1)S(1)}, u32[]{:S(2)}, u32[]{:S(2)}) collective-permute-start(bf16[384,384]{1,0:T(8,128)(2,1)} %slice.14), channel_id=1, source_target_pairs={{0,16},{16,32},{32,48},{48,64},{64,80},{80,96},{96,112},{112,128},... | collective-permute-start | bytes 884744 | tf_op jit(solution)/shard_map/ppermute | solution.py:92
  72.3 13.1 %collective-permute-start.6 = (bf16[384,384]{1,0:T(8,128)(2,1)}, bf16[384,384]{1,0:T(8,128)(2,1)S(1)}, u32[]{:S(2)}, u32[]{:S(2)}) collective-permute-start(bf16[384,384]{1,0:T(8,128)(2,1)} %slice.14), channel_id=1, source_target_pairs={{16,0},{32,16},{48,32},{64,48},{80,64},{96,80},{112,96},{128,112},... | collective-permute-start | bytes 884744 | tf_op jit(solution)/shard_map/ppermute | solution.py:92
  75.3 12.8 %collective-permute-start.7 = (bf16[384,384]{1,0:T(8,128)(2,1)}, bf16[384,384]{1,0:T(8,128)(2,1)S(1)}, u32[]{:S(2)}, u32[]{:S(2)}) collective-permute-start(bf16[384,384]{1,0:T(8,128)(2,1)} %slice.14), channel_id=1, source_target_pairs={{32,0},{48,16},{64,32},{80,48},{96,64},{112,80},{128,96},{144,112}... | collective-permute-start | bytes 884744 | tf_op jit(solution)/shard_map/ppermute | solution.py:92
Sparse Core Ops, SparseCore 0:
  36.4 89.6 all-gather.4
  127.8 81.0 all-gather.6

commit v3 on v1

--- a/solution.py
+++ b/solution.py
@@ -7,6 +7,7 @@
 from jax.experimental import pallas as pl
 from jax.experimental.pallas import tpu as pltpu
 from jax.sharding import PartitionSpec as P
+
 
 HD = 128
 BLK = 128
@@ -79,6 +80,9 @@
 
 def body(q_proj, k_proj, v_proj, gain_q, gain_k, tiles, *, n_frame):
     tok_rows, width = q_proj.shape
+    blocks = tok_rows // BLK
+    frame_pos = lax.axis_index("frame")
+
     q_wide = q_proj.astype(jnp.float32)
     k_wide = k_proj.astype(jnp.float32)
     row_sums = lax.psum(
@@ -91,27 +95,33 @@
     k_norm = (k_wide * lax.rsqrt(row_sums[1] / full_width + EPS)[:, None] * gain_k).astype(
         jnp.bfloat16
     )
-    blocks = tok_rows // BLK
-    frame_pos = lax.axis_index("frame")
     kv_pair = jnp.stack([k_norm, v_proj])
 
+    offsets = list(range(-NEAR, NEAR + 1))
     near = {0: kv_pair}
-    for d in range(-NEAR, NEAR + 1):
-        if d == 0:
-            continue
-        perm = [(i, i - d) for i in range(n_frame) if 0 <= i - d < n_frame]
-        near[d] = lax.ppermute(kv_pair, "frame", perm)
-    far = lax.all_gather(kv_pair[:, :BLK], "frame", axis=0, tiled=False)
+    for d in offsets:
+        if d != 0:
+            perm = [(i, i - d) for i in range(n_frame) if 0 <= i - d < n_frame]
+            near[d] = lax.ppermute(kv_pair, "frame", perm)
 
-    near_k = jnp.concatenate(
-        [near[d][0].reshape(blocks, BLK, width) for d in range(-NEAR, NEAR + 1)], axis=0
+    held = kv_pair[:, None, :BLK]
+    bit = 1
+    while bit < n_frame:
+        perm = [(i, i ^ bit) for i in range(n_frame)]
+        got = lax.ppermute(held, "frame", perm)
+        upper = (frame_pos // bit) % 2 == 1
+        held = jnp.where(
+            upper, jnp.concatenate([got, held], axis=1), jnp.concatenate([held, got], axis=1)
+        )
+        bit *= 2
+
+    k_bank = jnp.concatenate(
+        [near[d][0].reshape(blocks, BLK, width) for d in offsets] + [held[0]], axis=0
     )
-    near_v = jnp.concatenate(
-        [near[d][1].reshape(blocks, BLK, width) for d in range(-NEAR, NEAR + 1)], axis=0
+    v_bank = jnp.concatenate(
+        [near[d][1].reshape(blocks, BLK, width) for d in offsets] + [held[1]], axis=0
     )
-    k_bank = jnp.concatenate([near_k, far[:, 0]], axis=0)
-    v_bank = jnp.concatenate([near_v, far[:, 1]], axis=0)
-    n_near = (2 * NEAR + 1) * blocks
+    n_near = len(offsets) * blocks
 
     q_tiles = lax.dynamic_slice_in_dim(tiles, frame_pos * blocks, blocks, 0)
     key_slab = q_tiles // blocks

time: 175 us -> 214 us (1.22)
  the two profiles are of different devices: /device:TPU:64 before, /device:TPU:24 now
where the time goes in v3:
time: 214 us
  waiting for transfers between devices  104 us (49%)
  starting transfers between devices  51.3 us (24%)
  blocking collectives  33.7 us (16%)
  Pallas kernels  11.4 us (5%)
  local copies, waits for them, and re-layouts  6.93 us (3%)
  other arithmetic  6.68 us (3%)
    ppermute x4, waiting for transfers between devices, body(): got = lax.ppermute(held, 'frame', perm)  104 us
    ppermute x4, starting transfers between devices, body(): got = lax.ppermute(held, 'frame', perm)  36.4 us
    psum x1, blocking collectives, body(): lax.psum((jnp.sum(q_wide * q_wide, axis=1), jnp.sum(k_wide * k_wide, axis...  33.7 us
    ppermute x4, starting transfers between devices, body(): near[d] = lax.ppermute(kv_pair, 'frame', perm)  15 us
    pallas_call x1, Pallas kernels, sparse_attend(): pl.pallas_call(kernel, grid_spec=grid_spec, out_shape=jax.ShapeDtypeStruc...  11.4 us
  transfers between devices with their start and end apart: 8, of which 4 were waited for; matrix products, arithmetic and copies ran while one was open for 3% of the time, Pallas kernels for 0%

profile of v3, /device:TPU:24, one launch (start us, length us, event | category | flops | bytes accessed | tf_op | source)
XLA Modules:
  0.0 213.9 jit_solution(13267229175349188498)
XLA Ops:
  0.0 1.4 fusion.2
  1.5 33.7 %all-reduce = (f32[512]{0:T(512)}, f32[512]{0:T(512)S(1)}) all-reduce(f32[512]{0:T(512)S(1)} %get-tuple-element.17, f32[512]{0:T(512)S(1)} %get-tuple-element.18), channel_id=1, replica_groups=mesh['frame'=16,'tensor'=8,'dp'=2] {'tensor'}, use_global_device_ids=true, to_apply=%region_1.0 | all-reduce | flops 1024 | bytes 8192 | tf_op jit(solution)/shard_map/psum | solution.py:88
  35.2 1.2 fusion.19
  36.4 1.1 pad_maximum_fusion
  37.4 3.6 %collective-permute-start = (bf16[2,512,384]{2,1,0:T(8,128)(2,1)S(1)}, bf16[2,512,384]{2,1,0:T(8,128)(2,1)}, u32[]{:S(2)}, u32[]{:S(2)}) collective-permute-start(bf16[2,512,384]{2,1,0:T(8,128)(2,1)S(1)} %pad_maximum_fusion), channel_id=1, source_target_pairs={{0,32},{16,48},{32,64},{48,80},{64,96},{80,112},{96,128},{112,144}... | collective-permute-start | bytes 2359304 | tf_op jit(solution)/shard_map/ppermute | solution.py:105
  41.1 4.1 %collective-permute-start.1 = (bf16[2,512,384]{2,1,0:T(8,128)(2,1)S(1)}, bf16[2,512,384]{2,1,0:T(8,128)(2,1)}, u32[]{:S(2)}, u32[]{:S(2)}) collective-permute-start(bf16[2,512,384]{2,1,0:T(8,128)(2,1)S(1)} %pad_maximum_fusion), channel_id=1, source_target_pairs={{0,16},{16,32},{32,48},{48,64},{64,80},{80,96},{96,112},{112,128},... | collective-permute-start | bytes 2359304 | tf_op jit(solution)/shard_map/ppermute | solution.py:105
  45.2 1.9 collective-permute-start.2
  47.1 5.4 %collective-permute-start.3 = (bf16[2,512,384]{2,1,0:T(8,128)(2,1)S(1)}, bf16[2,512,384]{2,1,0:T(8,128)(2,1)S(1)}, u32[]{:S(2)}, u32[]{:S(2)}) collective-permute-start(bf16[2,512,384]{2,1,0:T(8,128)(2,1)S(1)} %pad_maximum_fusion), channel_id=1, source_target_pairs={{32,0},{48,16},{64,32},{80,48},{96,64},{112,80},{128,96},{144,112}... | collective-permute-start | bytes 2359304 | tf_op jit(solution)/shard_map/ppermute | solution.py:105
  52.5 0.9 fusion.9
  53.4 0.1 collective-permute-start.4
  53.5 0.2 fusion.7
  53.7 27.2 %collective-permute-done.4 = bf16[2,1,128,384]{3,2,1,0:T(8,128)(2,1)S(1)} collective-permute-done((bf16[2,1,128,384]{3,2,1,0:T(8,128)(2,1)S(1)}, bf16[2,1,128,384]{3,2,1,0:T(8,128)(2,1)S(1)}, u32[]{:S(2)}, u32[]{:S(2)}) %collective-permute-start.4) | collective-permute-done | bytes 196640 | tf_op jit(solution)/shard_map/ppermute | solution.py:111
  80.9 34.0 %collective-permute-start.5 = (bf16[2,2,128,384]{3,2,1,0:T(8,128)(2,1)S(1)}, bf16[2,2,128,384]{3,2,1,0:T(8,128)(2,1)S(1)}, u32[]{:S(2)}, u32[]{:S(2)}) collective-permute-start(bf16[2,2,128,384]{3,2,1,0:T(8,128)(2,1)S(1)} %maximum_select_fusion.3), channel_id=1, source_target_pairs={{0,32},{16,48},{32,0},{48,16},{64,96},{80,112},{96,64},{112,80},{1... | collective-permute-start | bytes 1179656 | tf_op jit(solution)/shard_map/ppermute | solution.py:111
  115.0 0.7 add_rsqrt_fusion.1
  115.6 0.2 fusion.4.q_ref
  115.8 0.1 constant_dynamic-slice_fusion
  115.9 0.1 copy.8
  116.0 4.7 %collective-permute-done.5 = bf16[2,2,128,384]{3,2,1,0:T(8,128)(2,1)S(1)} collective-permute-done((bf16[2,2,128,384]{3,2,1,0:T(8,128)(2,1)S(1)}, bf16[2,2,128,384]{3,2,1,0:T(8,128)(2,1)S(1)}, u32[]{:S(2)}, u32[]{:S(2)}) %collective-permute-start.5) | collective-permute-done | bytes 393248 | tf_op jit(solution)/shard_map/ppermute | solution.py:111
  120.7 0.1 maximum_select_fusion.2
  120.9 1.1 collective-permute-start.6
  122.0 1.2 fusion.18
  123.2 1.2 fusion.17
  124.4 13.4 %collective-permute-done.6 = bf16[2,4,128,384]{3,2,1,0:T(8,128)(2,1)S(1)} collective-permute-done((bf16[2,4,128,384]{3,2,1,0:T(8,128)(2,1)S(1)}, bf16[2,4,128,384]{3,2,1,0:T(8,128)(2,1)S(1)}, u32[]{:S(2)}, u32[]{:S(2)}) %collective-permute-start.6) | collective-permute-done | bytes 786464 | tf_op jit(solution)/shard_map/ppermute | solution.py:111
  137.8 0.3 maximum_select_fusion.1
  138.1 1.2 collective-permute-start.7
  139.5 1.2 fusion.16
  140.8 0.1 fusion.15
  141.2 58.2 %collective-permute-done.7 = bf16[2,8,128,384]{3,2,1,0:T(8,128)(2,1)S(1)} collective-permute-done((bf16[2,8,128,384]{3,2,1,0:T(8,128)(2,1)S(1)}, bf16[2,8,128,384]{3,2,1,0:T(8,128)(2,1)S(1)}, u32[]{:S(2)}, u32[]{:S(2)}) %collective-permute-start.7) | collective-permute-done | bytes 1572896 | tf_op jit(solution)/shard_map/ppermute | solution.py:111
  199.5 0.6 maximum_select_fusion
  200.1 0.7 fusion
  200.8 1.7 copy-done.1
  202.5 11.4 %shard_map.64 = bf16[512,384]{1,0:T(8,128)(2,1)} custom-call(s32[4,12]{1,0:T(4,128)S(1)} %fusion.12.idx_ref, bf16[512,384]{1,0:T(8,128)(2,1)S(1)} %fusion.4.q_ref, bf16[36,128,384]{2,1,0:T(8,128)(2,1)S(1)} %get-tuple-element.8.k_ref, bf16[36,128,384]{2,1,0:T(8,128)(2,1)} %copy-done.1), custom_call_target="tpu_custom_call" | custom-call | flops 1207959552 | bytes 7864320 | tf_op jit(solution)/shard_map/pallas_call | solution.py:68
  (30 shorter events, 0.7 us)
Async XLA Ops:
  0.0 115.8 %copy-start = (s32[64,12]{0,1:T(8,128)S(1)}, s32[64,12]{0,1:T(8,128)}, u32[]{:S(2)}) copy-start(s32[64,12]{0,1:T(8,128)} %param.11) | copy-start | bytes 9220
  0.0 115.6 %copy-start.4 = (bf16[512,384]{1,0:T(8,128)(2,1)S(1)}, bf16[512,384]{1,0:T(8,128)(2,1)}, u32[]{:S(2)}) copy-start(bf16[512,384]{1,0:T(8,128)(2,1)} %param.6) | copy-start | bytes 1179652
  0.0 53.5 %copy-start.2 = (bf16[512,384]{1,0:T(8,128)(2,1)S(1)}, bf16[512,384]{1,0:T(8,128)(2,1)}, u32[]{:S(2)}) copy-start(bf16[512,384]{1,0:T(8,128)(2,1)} %param.7) | copy-start | bytes 1179652
  0.0 53.5 %copy-start.5 = (f32[384]{0:T(512)S(1)}, f32[384]{0:T(512)}, u32[]{:S(2)}) copy-start(f32[384]{0:T(512)} %param.10) | copy-start | bytes 4612
  0.0 115.6 %copy-start.6 = (f32[384]{0:T(512)S(1)}, f32[384]{0:T(512)}, u32[]{:S(2)}) copy-start(f32[384]{0:T(512)} %param.9) | copy-start | bytes 4612
  37.4 84.5 %collective-permute-start = (bf16[2,512,384]{2,1,0:T(8,128)(2,1)S(1)}, bf16[2,512,384]{2,1,0:T(8,128)(2,1)}, u32[]{:S(2)}, u32[]{:S(2)}) collective-permute-start(bf16[2,512,384]{2,1,0:T(8,128)(2,1)S(1)} %pad_maximum_fusion), channel_id=1, source_target_pairs={{0,32},{16,48},{32,64},{48,80},{64,96},{80,112},{96,128},{112,144}... | collective-permute-start | bytes 2359304 | tf_op jit(solution)/shard_map/ppermute | solution.py:105
  41.1 82.2 %collective-permute-start.1 = (bf16[2,512,384]{2,1,0:T(8,128)(2,1)S(1)}, bf16[2,512,384]{2,1,0:T(8,128)(2,1)}, u32[]{:S(2)}, u32[]{:S(2)}) collective-permute-start(bf16[2,512,384]{2,1,0:T(8,128)(2,1)S(1)} %pad_maximum_fusion), channel_id=1, source_target_pairs={{0,16},{16,32},{32,48},{48,64},{64,80},{80,96},{96,112},{112,128},... | collective-permute-start | bytes 2359304 | tf_op jit(solution)/shard_map/ppermute | solution.py:105
  45.2 94.3 %collective-permute-start.2 = (bf16[2,512,384]{2,1,0:T(8,128)(2,1)S(1)}, bf16[2,512,384]{2,1,0:T(8,128)(2,1)}, u32[]{:S(2)}, u32[]{:S(2)}) collective-permute-start(bf16[2,512,384]{2,1,0:T(8,128)(2,1)S(1)} %pad_maximum_fusion), channel_id=1, source_target_pairs={{16,0},{32,16},{48,32},{64,48},{80,64},{96,80},{112,96},{128,112},... | collective-permute-start | bytes 2359304 | tf_op jit(solution)/shard_map/ppermute | solution.py:105
  47.1 93.7 %collective-permute-start.3 = (bf16[2,512,384]{2,1,0:T(8,128)(2,1)S(1)}, bf16[2,512,384]{2,1,0:T(8,128)(2,1)S(1)}, u32[]{:S(2)}, u32[]{:S(2)}) collective-permute-start(bf16[2,512,384]{2,1,0:T(8,128)(2,1)S(1)} %pad_maximum_fusion), channel_id=1, source_target_pairs={{32,0},{48,16},{64,32},{80,48},{96,64},{112,80},{128,96},{144,112}... | collective-permute-start | bytes 2359304 | tf_op jit(solution)/shard_map/ppermute | solution.py:105
  53.4 27.5 %collective-permute-start.4 = (bf16[2,1,128,384]{3,2,1,0:T(8,128)(2,1)S(1)}, bf16[2,1,128,384]{3,2,1,0:T(8,128)(2,1)S(1)}, u32[]{:S(2)}, u32[]{:S(2)}) collective-permute-start(bf16[2,1,128,384]{3,2,1,0:T(8,128)(2,1)S(1)} %fusion.9), channel_id=1, source_target_pairs={{0,16},{16,0},{32,48},{48,32},{64,80},{80,64},{96,112},{112,96},{1... | collective-permute-start | bytes 589832 | tf_op jit(solution)/shard_map/ppermute | solution.py:111
  80.9 39.8 %collective-permute-start.5 = (bf16[2,2,128,384]{3,2,1,0:T(8,128)(2,1)S(1)}, bf16[2,2,128,384]{3,2,1,0:T(8,128)(2,1)S(1)}, u32[]{:S(2)}, u32[]{:S(2)}) collective-permute-start(bf16[2,2,128,384]{3,2,1,0:T(8,128)(2,1)S(1)} %maximum_select_fusion.3), channel_id=1, source_target_pairs={{0,32},{16,48},{32,0},{48,16},{64,96},{80,112},{96,64},{112,80},{1... | collective-permute-start | bytes 1179656 | tf_op jit(solution)/shard_map/ppermute | solution.py:111
  120.9 17.0 %collective-permute-start.6 = (bf16[2,4,128,384]{3,2,1,0:T(8,128)(2,1)S(1)}, bf16[2,4,128,384]{3,2,1,0:T(8,128)(2,1)S(1)}, u32[]{:S(2)}, u32[]{:S(2)}) collective-permute-start(bf16[2,4,128,384]{3,2,1,0:T(8,128)(2,1)S(1)} %maximum_select_fusion.2), channel_id=1, source_target_pairs={{0,64},{16,80},{32,96},{48,112},{64,0},{80,16},{96,32},{112,48},{1... | collective-permute-start | bytes 2359304 | tf_op jit(solution)/shard_map/ppermute | solution.py:111
  138.1 61.4 %collective-permute-start.7 = (bf16[2,8,128,384]{3,2,1,0:T(8,128)(2,1)S(1)}, bf16[2,8,128,384]{3,2,1,0:T(8,128)(2,1)S(1)}, u32[]{:S(2)}, u32[]{:S(2)}) collective-permute-start(bf16[2,8,128,384]{3,2,1,0:T(8,128)(2,1)S(1)} %maximum_select_fusion.1), channel_id=1, source_target_pairs={{0,128},{16,144},{32,160},{48,176},{64,192},{80,208},{96,224},{112... | collective-permute-start | bytes 4718600 | tf_op jit(solution)/shard_map/ppermute | solution.py:111
  139.3 1.7 copy-start.3
  200.8 1.8 copy-start.1
